TPU v7x, 256 devices: a whole 4x4x8 slice. The times are simulated.
256 devices in a mesh: day: 8 (over x, core), row: 32 (over y, z).
Axes of the slice: x: 4, y: 4, z: 8, core: 2. Of those that a mesh axis runs over, the one named last changes fastest.
Arguments:
- features: bfloat16 [8, 768, 16, 128, 128], P('day', 'row'), may hold values from -6 to 6
- blocks: int32 [8, 768, 16], P('day', 'row'), may hold values from 0 to 255, as said below
- labels: int32 [8, 768, 128], P('day', 'row'), may hold values from 0 to 15
- coef: float32 [8, 16, 32768], P('day', None, 'row'), may hold values from -0.125 to 0.125
- direction: float32 [8, 16, 32768], P('day', None, 'row'), may hold values from -0.125 to 0.125
- prior: float32 [32768], P('row'), may hold values from 100 to 3000
Outputs:
- gradient: float32 [8, 16, 32768], P('day', None, 'row')
- hess_dir: float32 [8, 16, 32768], P('day', None, 'row')
Inputs may be any that keep to these rules, and one draw needn't show every extreme that they name: `blocks`: within one row tile the 16 block numbers are distinct.
All inputs are finite; a program needn't handle non-finite values.
Results may differ from a plain program's by a relative error of at most 0.0003.
Values may be sent and summed in bfloat16 or wider, within the bound.
No kernel may reach another device: no remote copies, remote signals or barrier semaphores. Data moves between devices by JAX's collectives and lax.ppermute only.
A program may use at most 64 MiB of HBM per device.

v0:
```python
import jax
import jax.numpy as jnp
from jax import lax
from jax.sharding import Mesh
from jax.sharding import PartitionSpec as P

ROW = ("row_0", "row_1")


def copy_for_each(value, axis):
    copies = jnp.broadcast_to(value, (lax.axis_size(axis), *value.shape))
    return lax.all_to_all(copies, axis, split_axis=0, concat_axis=0, tiled=True)


def extended(cells, sides, width):
    for axis, dim in sides:
        count = lax.axis_size(axis)
        ends = count - 1
        head = lax.slice_in_dim(cells, 0, width, axis=dim)
        tail = lax.slice_in_dim(cells, cells.shape[dim] - width, cells.shape[dim], axis=dim)
        cells = jnp.concatenate(
            [
                lax.ppermute(tail, axis, [(i, (i + 1) % count) for i in range(ends)]),
                cells,
                lax.ppermute(head, axis, [((i + 1) % count, i) for i in range(ends)]),
            ],
            axis=dim,
        )
    return cells


def scatter_axes(value, axes, dim):
    if not axes:
        return value
    nearer = lax.psum_scatter(value, axes[0], scatter_dimension=dim, tiled=True)
    return scatter_axes(nearer, axes[1:], dim)


def on_device(features, blocks, labels, coef, direction, prior):
    arms = coef.shape[1]
    width = features.shape[-1]
    coef_pair = jnp.concatenate([coef[0], direction[0]], axis=0).astype(jnp.bfloat16)
    local_blk = coef_pair.shape[1] // width
    by_block = coef_pair.reshape(2 * arms, local_blk, width).transpose(1, 0, 2)
    coef_table = lax.all_gather(by_block, "row_1", axis=0, tiled=True)
    coef_table = lax.all_gather(coef_table, "row_0", axis=0, tiled=True)
    nblk = coef_table.shape[0]
    both = jnp.concatenate([coef, direction], axis=1)
    neighbours = extended(both, (("day", 0),), 1)
    blks = blocks[0]
    selected = coef_table[blks]
    feats = features[0]
    logits_dir = jnp.einsum("tari,taki->tkr", feats, selected, preferred_element_type=jnp.float32)
    logits = logits_dir[:, :arms]
    lin_dir = logits_dir[:, arms:]
    expo = jnp.exp(logits)
    probs = expo / jnp.sum(expo, axis=1, keepdims=True)
    onehot = (labels[0][:, None, :] == jnp.arange(arms, dtype=jnp.int32)[None, :, None]).astype(
        jnp.float32
    )
    resid = probs - onehot
    hrow = probs * lin_dir - probs * jnp.sum(probs * lin_dir, axis=1, keepdims=True)
    both_low = jnp.concatenate([resid, hrow], axis=1).astype(jnp.bfloat16)
    contrib = jnp.einsum("tari,tkr->taki", feats, both_low, preferred_element_type=jnp.float32)
    contrib = contrib.reshape(-1, 2 * arms * width)
    top = lax.reduce_precision(contrib, exponent_bits=8, mantissa_bits=7)
    hi = top.astype(jnp.bfloat16)
    lo = (contrib - top).astype(jnp.bfloat16)
    outer = lax.axis_size("row_0")
    inner = lax.axis_size("row_1")
    order = jnp.arange(nblk, dtype=jnp.int32).reshape(outer, inner, -1).transpose(1, 0, 2)
    place = (order.reshape(-1)[:, None] == blks.reshape(-1)[None, :]).astype(jnp.bfloat16)
    split = jnp.einsum(
        "bp,jpc->jbc", place, jnp.stack([hi, lo], axis=0), preferred_element_type=jnp.float32
    )
    partial_terms = (split[0] + split[1]).reshape(nblk, 2 * arms, width)
    owned = lax.psum_scatter(partial_terms, "row_1", scatter_dimension=0, tiled=True)
    owned = lax.psum_scatter(owned, "row_0", scatter_dimension=0, tiled=True)
    owned = owned.transpose(1, 0, 2).reshape(2 * arms, -1)
    day_index = lax.axis_index("day")
    ndays = lax.axis_size("day")
    links = (day_index > 0).astype(jnp.float32) + (day_index < ndays - 1).astype(jnp.float32)
    coupling = links * neighbours[1] - neighbours[0] - neighbours[2]
    result = owned + prior[None, :] * coupling
    return (result[None, :arms], result[None, arms:])


def solution(mesh):
    finer = Mesh(mesh.devices.reshape(mesh.shape["day"], 4, 8), ("day", "row_0", "row_1"))
    return jax.shard_map(
        on_device,
        mesh=finer,
        in_specs=(
            P("day", ROW, None, None, None),
            P("day", ROW, None),
            P("day", ROW, None),
            P("day", None, ROW),
            P("day", None, ROW),
            P(ROW),
        ),
        out_specs=(P("day", None, ROW), P("day", None, ROW)),
        check_vma=False,
    )
```

profile of v0, /device:TPU:2, one launch (start us, length us, event | category | flops | bytes accessed | tf_op | source)
XLA Modules:
  0.0 209.9 jit_solution(5084960627540762023)
XLA Ops:
  7.2 0.0 all-gather.2.cloned.1.call-start
  7.2 0.9 constant_dynamic-update-slice_fusion.1
  8.1 0.9 constant_dynamic-update-slice_fusion
  9.1 30.9 %all_gather.6 = bf16[64,32,128]{2,1,0:T(8,128)(2,1)} all-gather(bf16[8,32,128]{2,1,0:T(8,128)(2,1)S(1)} %copy.30), channel_id=1, replica_groups=mesh['day'=8,'row_0'=4,'row_1'=8] {'row_1'}, dimensions={0}, use_global_device_ids=true | all-gather | bytes 589824 | tf_op jit(solution)/shard_map/all_gather | solution.py:45
  40.0 0.0 all-gather.2.cloned.1.call-update
  40.1 0.0 reduce-scatter.3.cloned.1.call-start
  40.1 0.8 copy.34
  40.9 0.7 compare_select_fusion
  41.6 0.1 copy.31
  41.7 0.1 reshape.141
  41.8 0.1 reshape.137
  41.9 0.1 eq.35
  41.9 31.2 %all-gather.2.cloned.1.call-done = bf16[256,32,128]{2,1,0:T(8,128)(2,1)} async-done(((bf16[64,32,128]{2,1,0:T(8,128)(2,1)}), bf16[256,32,128]{2,1,0:T(8,128)(2,1)}) %all-gather.2.cloned.1.call-update) | async-done | bytes 2097168 | tf_op jit(solution)/shard_map/all_gather | solution.py:46
  73.1 2.8 %gather_fusion = bf16[384,32,128]{2,1,0:T(8,128)(2,1)S(1)} fusion(bf16[256,32,128]{2,1,0:T(8,128)(2,1)} %all-gather.2.cloned.1.call-done, s32[1024]{0:T(1024)S(1)} %pad_clamp_fusion), kind=kCustom, calls=%fused_computation | custom fusion | bytes 6292992 | tf_op jit(solution)/shard_map/gather | solution.py:51
  76.0 0.0 copy-start.1
  76.0 7.0 %fusion.13 = f32[24,32,128]{2,1,0:T(8,128)S(1)} fusion(bf16[24,16,32,128]{3,2,1,0:T(8,128)(2,1)S(1)} %bitcast.59, bf16[1,24,16,128,128]{4,3,2,1,0:T(8,128)(2,1)} %param.6), kind=kOutput, calls=%fused_computation.16 | convolution fusion | flops 402653184 | bytes 16121856 | tf_op jit(solution)/shard_map/tari,taki->tkr/dot_general | solution.py:53
  83.0 0.0 copy-done.1
  83.0 0.8 subtract_convert_fusion
  83.8 0.1 fusion.19
  83.8 9.0 %fusion.10 = f32[24,16,32,128]{3,2,1,0:T(8,128)} fusion(bf16[1,24,16,128,128]{4,3,2,1,0:T(8,128)(2,1)} %param.6, bf16[24,16,128]{2,1,0:T(8,128)(2,1)S(1)} %fusion.19, bf16[24,16,128]{2,1,0:T(8,128)(2,1)S(1)} %get-tuple-element.10), kind=kOutput, calls=%fused_computation.15 | convolution fusion | flops 403046400 | bytes 19070976 | tf_op jit(solution)/shard_map/tari,tkr->taki/dot_general | solution.py:64
  92.8 7.2 %reshape.130 = f32[1,384,4096]{2,1,0:T(8,128)} reshape(f32[24,16,32,128]{3,2,1,0:T(8,128)} %fusion.10) | data formatting | bytes 12582912 | tf_op jit(solution)/shard_map/reshape | solution.py:65
  100.0 6.6 %copy.32 = f32[1,384,4096]{1,2,0:T(8,128)} copy(f32[1,384,4096]{2,1,0:T(8,128)} %reshape.130) | data formatting | bytes 12582912 | tf_op jit(solution)/shard_map/reshape | solution.py:65
  106.6 3.8 %reduce-precision_convert_fusion = (bf16[1,384,4096]{1,2,0:T(8,128)(2,1)S(1)}, bf16[1,384,4096]{1,2,0:T(8,128)(2,1)S(1)}) fusion(f32[1,384,4096]{1,2,0:T(8,128)} %copy.32), kind=kLoop, calls=%fused_computation.8 | loop fusion | flops 6291456 | bytes 12582912 | tf_op jit(solution)/shard_map/convert_element_type | solution.py:67
  110.3 2.4 %convolution_bitcast_fusion = f32[2,256,4096]{1,2,0:T(8,128)S(1)} fusion(bf16[1,384,4096]{1,2,0:T(8,128)(2,1)S(1)} %get-tuple-element.3, bf16[1,384,4096]{1,2,0:T(8,128)(2,1)S(1)} %get-tuple-element.2, s32[384]{0:T(512)S(1)} %eq.35, s32[256]{0:T(256)S(1)} %reshape.137), kind=kOutput, calls=%fused_computation.9 | convolution fusion | flops 1613856768 | bytes 14682624 | tf_op jit(solution)/shard_map/bp,jpc->jbc/dot_general | solution.py:73
  112.8 2.5 %slice_add_fusion = f32[1,256,4096]{1,2,0:T(8,128)} fusion(f32[2,256,4096]{1,2,0:T(8,128)S(1)} %convolution_bitcast_fusion), kind=kLoop, calls=%fused_computation.14 | loop fusion | flops 1048576 | bytes 12582912 | tf_op jit(solution)/shard_map/add | solution.py:76
  115.3 5.5 %copy.35 = f32[256,32,128]{2,1,0:T(8,128)} copy(f32[256,32,128]{0,2,1:T(8,128)} %bitcast.58) | data formatting | bytes 8388608 | tf_op jit(solution)/shard_map/add | solution.py:76
  120.8 0.0 copy-start
  120.8 0.0 reduce-scatter.3.cloned.1.call-update
  120.8 0.0 reduce-scatter.5.cloned.1.call-start
  120.8 55.5 %reduce-scatter.3.cloned.1.call-done = f32[32,32,128]{2,1,0:T(8,128)} async-done(((f32[256,32,128]{2,1,0:T(8,128)}), f32[32,32,128]{2,1,0:T(8,128)}) %reduce-scatter.3.cloned.1.call-update) | async-done | bytes 524304 | tf_op jit(solution)/shard_map/reduce_scatter | solution.py:77
  176.3 0.0 reduce-scatter.5.cloned.1.call-update
  176.3 1.9 collective-permute-start
  178.3 3.6 %collective-permute-start.1 = (f32[1,32,1024]{2,1,0:T(8,128)S(1)}, f32[1,32,1024]{2,1,0:T(8,128)S(1)}, u32[]{:S(2)}, u32[]{:S(2)}) collective-permute-start(f32[1,32,1024]{2,1,0:T(8,128)S(1)} %get-tuple-element.6), channel_id=1, source_target_pairs={{32,0},{64,32},{96,64},{128,96},{160,128},{192,160},{224,192},{33,... | collective-permute-start | bytes 393224 | tf_op jit(solution)/shard_map/ppermute | solution.py:25
  181.9 0.7 collective-permute-done
  182.6 1.8 collective-permute-done.1
  184.4 17.3 %reduce-scatter.5.cloned.1.call-done = f32[8,32,128]{2,1,0:T(8,128)} async-done(((f32[32,32,128]{2,1,0:T(8,128)}), f32[8,32,128]{2,1,0:T(8,128)}) %reduce-scatter.5.cloned.1.call-update) | async-done | bytes 131088 | tf_op jit(solution)/shard_map/reduce_scatter | solution.py:78
  201.7 0.0 copy-done
  201.7 0.9 bitcast_add_fusion
  202.7 0.7 slice_bitcast_fusion
  (6 shorter events, 0.0 us)
Async XLA Ops:
  7.2 66.0 %all-gather.2.cloned.1.call-start = ((), (), s32[]{:S(2)}) async-start(), calls=%async_computation.2 | async-start | bytes 2621440 | tf_op jit(solution)/shard_map/all_gather | solution.py:46
  40.1 136.2 %reduce-scatter.3.cloned.1.call-start = ((), (), s32[]{:S(2)}) async-start(), calls=%async_computation.3 | async-start | bytes 4718592 | tf_op jit(solution)/shard_map/reduce_scatter | solution.py:77
  76.0 7.0 %copy-start.1 = (s32[1,24,128]{2,1,0:T(8,128)S(1)}, s32[1,24,128]{2,1,0:T(8,128)}, u32[]{:S(2)}) copy-start(s32[1,24,128]{2,1,0:T(8,128)} %param.8) | copy-start | bytes 36868
  120.8 81.0 %copy-start = (f32[1024]{0:T(1024)S(1)}, f32[1024]{0:T(1024)}, u32[]{:S(2)}) copy-start(f32[1024]{0:T(1024)} %param.11) | copy-start | bytes 12292
  120.8 80.9 %reduce-scatter.5.cloned.1.call-start = ((), (), s32[]{:S(2)}) async-start(), calls=%async_computation.4 | async-start | bytes 655360 | tf_op jit(solution)/shard_map/reduce_scatter | solution.py:78
  176.3 6.3 %collective-permute-start = (f32[1,32,1024]{2,1,0:T(8,128)S(1)}, f32[1,32,1024]{2,1,0:T(8,128)S(1)}, u32[]{:S(2)}, u32[]{:S(2)}) collective-permute-start(f32[1,32,1024]{2,1,0:T(8,128)S(1)} %get-tuple-element.6), channel_id=1, source_target_pairs={{0,32},{32,64},{64,96},{96,128},{128,160},{160,192},{192,224},{1,3... | collective-permute-start | bytes 393224 | tf_op jit(solution)/shard_map/ppermute | solution.py:23
  178.3 6.1 %collective-permute-start.1 = (f32[1,32,1024]{2,1,0:T(8,128)S(1)}, f32[1,32,1024]{2,1,0:T(8,128)S(1)}, u32[]{:S(2)}, u32[]{:S(2)}) collective-permute-start(f32[1,32,1024]{2,1,0:T(8,128)S(1)} %get-tuple-element.6), channel_id=1, source_target_pairs={{32,0},{64,32},{96,64},{128,96},{160,128},{192,160},{224,192},{33,... | collective-permute-start | bytes 393224 | tf_op jit(solution)/shard_map/ppermute | solution.py:25
Sparse Core Ops, SparseCore 0:
  40.2 32.8 all-gather.1
  120.9 55.3 reduce-scatter.2
  178.8 22.8 reduce-scatter.4
where the time goes:
time: 211 us; the launch traced here: 210 us
  waiting for transfers between devices  107 us (51%)
  blocking collectives  30.9 us (15%)
  local copies, waits for them, and re-layouts  23.8 us (11%)
  matrix products  18.5 us (9%)
  between operations  13.9 us (7%)
  other arithmetic  10.6 us (5%)
  starting transfers between devices  5.68 us (3%)
    reduce_scatter x1, waiting for transfers between devices, on_device(): lax.psum_scatter(partial_terms, 'row_1', scatter_dimension=0, tiled=True)  55.5 us
    all_gather x1, waiting for transfers between devices, on_device(): coef_table = lax.all_gather(coef_table, 'row_0', axis=0, tiled=True)  31.2 us
    all_gather x1, blocking collectives, on_device(): coef_table = lax.all_gather(by_block, 'row_1', axis=0, tiled=True)  30.9 us
    reduce_scatter x1, waiting for transfers between devices, on_device(): owned = lax.psum_scatter(owned, 'row_0', scatter_dimension=0, tiled=True)  17.3 us
    reshape x2, local copies, waits for them, and re-layouts, on_device(): contrib = contrib.reshape(-1, 2 * arms * width)  13.7 us
    dot_general x1, matrix products, on_device(): jnp.einsum('tari,tkr->taki', feats, both_low, preferred_element_type=jnp....  8.99 us
    dot_general x1, matrix products, on_device(): jnp.einsum('tari,taki->tkr', feats, selected, preferred_element_type=jnp....  7.03 us
    add x1, local copies, waits for them, and re-layouts, on_device(): partial_terms = (split[0] + split[1]).reshape(nblk, 2 * arms, width)  5.49 us
  transfers between devices with their start and end apart: 5, of which 5 were waited for; matrix products, arithmetic and copies ran while one was open for 1% of the time, Pallas kernels for 0%

commit v1 on v0

--- a/solution.py
+++ b/solution.py
@@ -42,7 +42,9 @@
     coef_pair = jnp.concatenate([coef[0], direction[0]], axis=0).astype(jnp.bfloat16)
     local_blk = coef_pair.shape[1] // width
     by_block = coef_pair.reshape(2 * arms, local_blk, width).transpose(1, 0, 2)
-    coef_table = lax.all_gather(by_block, "row_1", axis=0, tiled=True)
+    coef_table = jnp.concatenate(
+        lax.all_to_all(jnp.stack([by_block] * lax.axis_size("row_1")), "row_1", 0, 0), axis=0
+    )
     coef_table = lax.all_gather(coef_table, "row_0", axis=0, tiled=True)
     nblk = coef_table.shape[0]
     both = jnp.concatenate([coef, direction], axis=1)

time: 211 us -> 202 us (0.957)
  blocking collectives: 30.9 us -> 25.9 us
  waiting for transfers between devices: 107 us -> 103 us
    all_gather x1 -> x0, blocking collectives: 30.9 us -> none  [on_device(): coef_table = lax.all_gather(by_block, 'row_1', axis=0, tiled=True)]
    all_to_all x0 -> x1, blocking collectives: none -> 25.9 us  [on_device(): lax.all_to_all(jnp.stack([by_block] * lax.axis_size('row_1')), 'row_1', 0...]
    all_gather x1, waiting for transfers between devices: 31.2 us -> 27.9 us  [on_device(): coef_table = lax.all_gather(coef_table, 'row_0', axis=0, tiled=True)]
where the time goes in v1:
time: 202 us
  waiting for transfers between devices  103 us (51%)
  blocking collectives  25.9 us (13%)
  local copies, waits for them, and re-layouts  23.9 us (12%)
  matrix products  18.5 us (9%)
  between operations  13.9 us (7%)
  other arithmetic  10.6 us (5%)
  starting transfers between devices  5.68 us (3%)
    reduce_scatter x1, waiting for transfers between devices, on_device(): lax.psum_scatter(partial_terms, 'row_1', scatter_dimension=0, tiled=True)  55.5 us
    all_gather x1, waiting for transfers between devices, on_device(): coef_table = lax.all_gather(coef_table, 'row_0', axis=0, tiled=True)  27.9 us
    all_to_all x1, blocking collectives, on_device(): lax.all_to_all(jnp.stack([by_block] * lax.axis_size('row_1')), 'row_1', 0...  25.9 us
    reduce_scatter x1, waiting for transfers between devices, on_device(): owned = lax.psum_scatter(owned, 'row_0', scatter_dimension=0, tiled=True)  17.3 us
    reshape x2, local copies, waits for them, and re-layouts, on_device(): contrib = contrib.reshape(-1, 2 * arms * width)  13.7 us
    dot_general x1, matrix products, on_device(): jnp.einsum('tari,tkr->taki', feats, both_low, preferred_element_type=jnp....  8.99 us
    dot_general x1, matrix products, on_device(): jnp.einsum('tari,taki->tkr', feats, selected, preferred_element_type=jnp....  7.03 us
    add x1, local copies, waits for them, and re-layouts, on_device(): partial_terms = (split[0] + split[1]).reshape(nblk, 2 * arms, width)  5.49 us
  transfers between devices with their start and end apart: 5, of which 5 were waited for; matrix products, arithmetic and copies ran while one was open for 1% of the time, Pallas kernels for 0%

profile of v1, /device:TPU:2, one launch (start us, length us, event | category | flops | bytes accessed | tf_op | source)
XLA Modules:
  0.0 201.7 jit_solution(490100856579530954)
XLA Ops:
  7.2 0.0 all-gather.2.cloned.1.call-start
  7.2 0.9 constant_dynamic-update-slice_fusion.1
  8.1 0.9 constant_dynamic-update-slice_fusion
  9.1 0.1 stack.4
  9.2 25.9 %all_to_all.5 = bf16[8,8,32,128]{3,2,1,0:T(8,128)(2,1)} all-to-all(bf16[8,8,32,128]{3,2,1,0:T(8,128)(2,1)S(1)} %stack.4), channel_id=1, replica_groups=mesh['day'=8,'row_0'=4,'row_1'=8] {'row_1'}, dimensions={0} | all-to-all | bytes 1048576 | tf_op jit(solution)/shard_map/all_to_all | solution.py:46
  35.1 0.0 all-gather.2.cloned.1.call-update
  35.1 0.0 reduce-scatter.3.cloned.1.call-start
  35.2 0.8 copy.28
  35.9 0.7 compare_select_fusion
  36.6 0.1 copy.25
  36.7 0.1 reshape.147
  36.8 0.1 reshape.143
  36.9 0.1 eq.35
  37.0 27.9 %all-gather.2.cloned.1.call-done = bf16[256,32,128]{2,1,0:T(8,128)(2,1)} async-done(((bf16[64,32,128]{2,1,0:T(8,128)(2,1)}), bf16[256,32,128]{2,1,0:T(8,128)(2,1)}) %all-gather.2.cloned.1.call-update) | async-done | bytes 2097168 | tf_op jit(solution)/shard_map/all_gather | solution.py:48
  64.9 2.8 %gather_fusion = bf16[384,32,128]{2,1,0:T(8,128)(2,1)S(1)} fusion(bf16[256,32,128]{2,1,0:T(8,128)(2,1)} %all-gather.2.cloned.1.call-done, s32[1024]{0:T(1024)S(1)} %pad_clamp_fusion), kind=kCustom, calls=%fused_computation | custom fusion | bytes 6292992 | tf_op jit(solution)/shard_map/gather | solution.py:53
  67.8 0.0 copy-start.1
  67.8 7.0 %fusion.13 = f32[24,32,128]{2,1,0:T(8,128)S(1)} fusion(bf16[24,16,32,128]{3,2,1,0:T(8,128)(2,1)S(1)} %bitcast.60, bf16[1,24,16,128,128]{4,3,2,1,0:T(8,128)(2,1)} %param.6), kind=kOutput, calls=%fused_computation.16 | convolution fusion | flops 402653184 | bytes 16121856 | tf_op jit(solution)/shard_map/tari,taki->tkr/dot_general | solution.py:55
  74.8 0.0 copy-done.1
  74.8 0.8 subtract_convert_fusion
  75.6 0.1 fusion.19
  75.7 9.0 %fusion.10 = f32[24,16,32,128]{3,2,1,0:T(8,128)} fusion(bf16[1,24,16,128,128]{4,3,2,1,0:T(8,128)(2,1)} %param.6, bf16[24,16,128]{2,1,0:T(8,128)(2,1)S(1)} %fusion.19, bf16[24,16,128]{2,1,0:T(8,128)(2,1)S(1)} %get-tuple-element.10), kind=kOutput, calls=%fused_computation.15 | convolution fusion | flops 403046400 | bytes 19070976 | tf_op jit(solution)/shard_map/tari,tkr->taki/dot_general | solution.py:66
  84.7 7.2 %reshape.136 = f32[1,384,4096]{2,1,0:T(8,128)} reshape(f32[24,16,32,128]{3,2,1,0:T(8,128)} %fusion.10) | data formatting | bytes 12582912 | tf_op jit(solution)/shard_map/reshape | solution.py:67
  91.8 6.6 %copy.26 = f32[1,384,4096]{1,2,0:T(8,128)} copy(f32[1,384,4096]{2,1,0:T(8,128)} %reshape.136) | data formatting | bytes 12582912 | tf_op jit(solution)/shard_map/reshape | solution.py:67
  98.4 3.8 %reduce-precision_convert_fusion = (bf16[1,384,4096]{1,2,0:T(8,128)(2,1)S(1)}, bf16[1,384,4096]{1,2,0:T(8,128)(2,1)S(1)}) fusion(f32[1,384,4096]{1,2,0:T(8,128)} %copy.26), kind=kLoop, calls=%fused_computation.8 | loop fusion | flops 6291456 | bytes 12582912 | tf_op jit(solution)/shard_map/convert_element_type | solution.py:69
  102.1 2.4 %convolution_bitcast_fusion = f32[2,256,4096]{1,2,0:T(8,128)S(1)} fusion(bf16[1,384,4096]{1,2,0:T(8,128)(2,1)S(1)} %get-tuple-element.3, bf16[1,384,4096]{1,2,0:T(8,128)(2,1)S(1)} %get-tuple-element.2, s32[384]{0:T(512)S(1)} %eq.35, s32[256]{0:T(256)S(1)} %reshape.143), kind=kOutput, calls=%fused_computation.9 | convolution fusion | flops 1613856768 | bytes 14682624 | tf_op jit(solution)/shard_map/bp,jpc->jbc/dot_general | solution.py:75
  104.6 2.5 %slice_add_fusion = f32[1,256,4096]{1,2,0:T(8,128)} fusion(f32[2,256,4096]{1,2,0:T(8,128)S(1)} %convolution_bitcast_fusion), kind=kLoop, calls=%fused_computation.14 | loop fusion | flops 1048576 | bytes 12582912 | tf_op jit(solution)/shard_map/add | solution.py:78
  107.1 5.5 %copy.29 = f32[256,32,128]{2,1,0:T(8,128)} copy(f32[256,32,128]{0,2,1:T(8,128)} %bitcast.59) | data formatting | bytes 8388608 | tf_op jit(solution)/shard_map/add | solution.py:78
  112.6 0.0 copy-start
  112.6 0.0 reduce-scatter.3.cloned.1.call-update
  112.6 0.0 reduce-scatter.5.cloned.1.call-start
  112.7 55.5 %reduce-scatter.3.cloned.1.call-done = f32[32,32,128]{2,1,0:T(8,128)} async-done(((f32[256,32,128]{2,1,0:T(8,128)}), f32[32,32,128]{2,1,0:T(8,128)}) %reduce-scatter.3.cloned.1.call-update) | async-done | bytes 524304 | tf_op jit(solution)/shard_map/reduce_scatter | solution.py:79
  168.1 0.0 reduce-scatter.5.cloned.1.call-update
  168.2 1.9 collective-permute-start
  170.1 3.6 %collective-permute-start.1 = (f32[1,32,1024]{2,1,0:T(8,128)S(1)}, f32[1,32,1024]{2,1,0:T(8,128)S(1)}, u32[]{:S(2)}, u32[]{:S(2)}) collective-permute-start(f32[1,32,1024]{2,1,0:T(8,128)S(1)} %get-tuple-element.6), channel_id=1, source_target_pairs={{32,0},{64,32},{96,64},{128,96},{160,128},{192,160},{224,192},{33,... | collective-permute-start | bytes 393224 | tf_op jit(solution)/shard_map/ppermute | solution.py:25
  173.8 0.7 collective-permute-done
  174.5 1.8 collective-permute-done.1
  176.2 17.3 %reduce-scatter.5.cloned.1.call-done = f32[8,32,128]{2,1,0:T(8,128)} async-done(((f32[32,32,128]{2,1,0:T(8,128)}), f32[8,32,128]{2,1,0:T(8,128)}) %reduce-scatter.5.cloned.1.call-update) | async-done | bytes 131088 | tf_op jit(solution)/shard_map/reduce_scatter | solution.py:80
  193.5 0.0 copy-done
  193.5 0.9 bitcast_add_fusion
  194.5 0.7 slice_bitcast_fusion
  (6 shorter events, 0.0 us)
Async XLA Ops:
  7.2 57.8 %all-gather.2.cloned.1.call-start = ((), (), s32[]{:S(2)}) async-start(), calls=%async_computation.3 | async-start | bytes 2621440 | tf_op jit(solution)/shard_map/all_gather | solution.py:48
  35.1 133.0 %reduce-scatter.3.cloned.1.call-start = ((), (), s32[]{:S(2)}) async-start(), calls=%async_computation.4 | async-start | bytes 4718592 | tf_op jit(solution)/shard_map/reduce_scatter | solution.py:79
  67.8 7.0 %copy-start.1 = (s32[1,24,128]{2,1,0:T(8,128)S(1)}, s32[1,24,128]{2,1,0:T(8,128)}, u32[]{:S(2)}) copy-start(s32[1,24,128]{2,1,0:T(8,128)} %param.8) | copy-start | bytes 36868
  112.6 80.9 %copy-start = (f32[1024]{0:T(1024)S(1)}, f32[1024]{0:T(1024)}, u32[]{:S(2)}) copy-start(f32[1024]{0:T(1024)} %param.11) | copy-start | bytes 12292
  112.6 80.9 %reduce-scatter.5.cloned.1.call-start = ((), (), s32[]{:S(2)}) async-start(), calls=%async_computation.5 | async-start | bytes 655360 | tf_op jit(solution)/shard_map/reduce_scatter | solution.py:80
  168.2 6.3 %collective-permute-start = (f32[1,32,1024]{2,1,0:T(8,128)S(1)}, f32[1,32,1024]{2,1,0:T(8,128)S(1)}, u32[]{:S(2)}, u32[]{:S(2)}) collective-permute-start(f32[1,32,1024]{2,1,0:T(8,128)S(1)} %get-tuple-element.6), channel_id=1, source_target_pairs={{0,32},{32,64},{64,96},{96,128},{128,160},{160,192},{192,224},{1,3... | collective-permute-start | bytes 393224 | tf_op jit(solution)/shard_map/ppermute | solution.py:23
  170.1 6.1 %collective-permute-start.1 = (f32[1,32,1024]{2,1,0:T(8,128)S(1)}, f32[1,32,1024]{2,1,0:T(8,128)S(1)}, u32[]{:S(2)}, u32[]{:S(2)}) collective-permute-start(f32[1,32,1024]{2,1,0:T(8,128)S(1)} %get-tuple-element.6), channel_id=1, source_target_pairs={{32,0},{64,32},{96,64},{128,96},{160,128},{192,160},{224,192},{33,... | collective-permute-start | bytes 393224 | tf_op jit(solution)/shard_map/ppermute | solution.py:25
Sparse Core Ops, SparseCore 0:
  35.2 29.6 all-gather.1
  112.7 55.3 reduce-scatter.2
  170.7 22.8 reduce-scatter.4
